TPU v7x, 512 devices: a whole 4x4x16 slice. The times are simulated.
512 devices in a mesh: ctx: 64 (over x, y, z_hi, core), head: 8 (over z_lo).
Axes of the slice: x: 4, y: 4, z: 16 (z_hi: 2, z_lo: 8; z = z_hi * 8 + z_lo), core: 2. Of those that a mesh axis runs over, the one named last changes fastest.
Arguments:
- query_head_rows: bfloat16 [16384, 4096], P('ctx', 'head'), may hold values from -4 to 4
- key_head_rows: bfloat16 [16384, 1024], P('ctx', 'head'), may hold values from -4 to 4
- value_head_rows: bfloat16 [16384, 1024], P('ctx', 'head'), may hold values from -4 to 4
- forward_output: bfloat16 [16384, 4096], P('ctx', 'head'), may hold values from -4 to 4, as said below
- cotangent: bfloat16 [16384, 4096], P('ctx', 'head'), may hold values from -6 to 6
- logsumexp: float32 [32, 16384], P('head', 'ctx'), as said below
- document_lengths: int32 [64], replicated, may hold values from 1 to 768, as said below
- linear_row_index: int32 [16384], replicated, may hold values from 0 to 16383, as said below
Outputs:
- query_gradient: bfloat16 [16384, 4096], P(('ctx', 'head'))
- linear_key_gradient: bfloat16 [16384, 1024], P(('ctx', 'head'))
- linear_value_gradient: bfloat16 [16384, 1024], P(('ctx', 'head'))
Inputs may be any that keep to these rules, and one draw needn't show every extreme that they name: `logsumexp`: for each head and position, the log of the sum of exp(scores) over the keys that the position sees, from the forward pass on these query_head_rows and key_head_rows. `forward_output`: for each head, the forward pass's softmax weights times value_head_rows, rounded to bfloat16. `document_lengths`: the lengths sum to 16384; the longest document has exactly 768 tokens. `linear_row_index`: A permutation of the 16384 positions. Counting positions in blocks of 256, from one block of the packed sequence at most 8 rows go to one block of linear positions, some pair of blocks reaches 8, and every linear block receives 256 rows.
All inputs are finite; a program needn't handle non-finite values.
Results may differ from a plain program's by a relative error of at most 0.0049.
Values may be sent and summed in bfloat16 or wider, within the bound.
No kernel may reach another device: no remote copies, remote signals or barrier semaphores. Data moves between devices by JAX's collectives and lax.ppermute only.
A program may use at most 64 MiB of HBM per device.

v0:
```python
import jax
import jax.numpy as jnp
from jax import lax
from jax.sharding import PartitionSpec as P

HEAD_SIZE = 128
DOC_BLOCKS = 3


def from_behind(shard, axis, by):
    count = lax.axis_size(axis)
    pairs = [(i, i + by) for i in range(count) if 0 <= i + by < count]
    return lax.ppermute(shard, axis, pairs)


def shifted(block, axis, distance):
    devices = range(lax.axis_size(axis))
    route = [((i - distance) % len(devices), i) for i in devices]
    return lax.ppermute(block, axis, route)


def block_grads(
    query_vectors,
    output_gradient,
    log_normalizer,
    row_correction,
    begins,
    query_pos,
    key_part,
    value_part,
    key_start,
):
    length = query_vectors.shape[0]
    kv_heads = query_vectors.shape[1]
    scaling = HEAD_SIZE ** (-0.5)
    key_heads = key_part.reshape(length, kv_heads, HEAD_SIZE)
    value_heads = value_part.reshape(length, kv_heads, HEAD_SIZE)
    scores = (
        jnp.einsum("qngd,knd->qngk", query_vectors, key_heads, preferred_element_type=jnp.float32)
        * scaling
    )
    key_pos = key_start + lax.iota(jnp.int32, length)
    visible = (key_pos[None, :] <= query_pos[:, None]) & (key_pos[None, :] >= begins[:, None])
    weights = jnp.exp(
        jnp.where(visible[:, None, None, :], scores - log_normalizer[..., None], -jnp.inf)
    )
    weights_low = weights.astype(jnp.bfloat16)
    grad_weights = jnp.einsum(
        "qngd,knd->qngk", output_gradient, value_heads, preferred_element_type=jnp.float32
    )
    grad_scores = (weights * (grad_weights - row_correction[..., None]) * scaling).astype(
        jnp.bfloat16
    )
    query_term = jnp.einsum(
        "qngk,knd->qngd", grad_scores, key_heads, preferred_element_type=jnp.float32
    )
    key_term = jnp.einsum(
        "qngk,qngd->knd", grad_scores, query_vectors, preferred_element_type=jnp.float32
    )
    value_term = jnp.einsum(
        "qngk,qngd->knd", weights_low, output_gradient, preferred_element_type=jnp.float32
    )
    return (query_term, key_term.reshape(length, -1), value_term.reshape(length, -1))


def per_device(
    query_head_rows,
    key_head_rows,
    value_head_rows,
    forward_output,
    cotangent,
    logsumexp,
    document_lengths,
    linear_row_index,
):
    length = query_head_rows.shape[0]
    kv_heads = key_head_rows.shape[1] // HEAD_SIZE
    query_groups = logsumexp.shape[0] // kv_heads
    block_index = lax.axis_index("ctx")
    blocks = lax.axis_size("ctx")
    query_pos = block_index * length + lax.iota(jnp.int32, length)
    finish = jnp.cumsum(document_lengths)
    firsts = finish - document_lengths
    begins = jnp.max(jnp.where(firsts[None, :] <= query_pos[:, None], firsts[None, :], 0), axis=1)
    query_vectors = query_head_rows.reshape(length, kv_heads, query_groups, HEAD_SIZE)
    output_gradient = cotangent.reshape(length, kv_heads, query_groups, HEAD_SIZE)
    log_normalizer = logsumexp.T.reshape(length, kv_heads, query_groups)
    row_correction = jnp.sum(
        output_gradient.astype(jnp.float32)
        * forward_output.reshape(length, kv_heads, query_groups, HEAD_SIZE).astype(jnp.float32),
        axis=3,
    )

    def block_terms(key_part, value_part, distance):
        key_start = (block_index - distance) * length
        return block_grads(
            query_vectors,
            output_gradient,
            log_normalizer,
            row_correction,
            begins,
            query_pos,
            key_part,
            value_part,
            key_start,
        )

    query_acc, key_running_sum, value_running_sum = block_terms(key_head_rows, value_head_rows, 0)
    moving_keys, moving_values = (key_head_rows, value_head_rows)
    for distance in range(1, DOC_BLOCKS + 1):
        moving_keys, moving_values = from_behind((moving_keys, moving_values), "ctx", 1)
        key_running_sum, value_running_sum = shifted((key_running_sum, value_running_sum), "ctx", 1)
        query_term, key_term, value_term = block_terms(moving_keys, moving_values, distance)
        query_acc = query_acc + query_term
        key_running_sum = key_running_sum + key_term
        value_running_sum = value_running_sum + value_term
    key_running_sum, value_running_sum = (
        shifted(key_running_sum.astype(jnp.bfloat16), "ctx", -DOC_BLOCKS).astype(
            key_running_sum.dtype
        ),
        shifted(value_running_sum.astype(jnp.bfloat16), "ctx", -DOC_BLOCKS).astype(
            value_running_sum.dtype
        ),
    )
    query_grad = query_acc.reshape(length, -1).astype(jnp.bfloat16)
    key_row_gradient = key_running_sum.astype(jnp.bfloat16)
    value_row_gradient = value_running_sum.astype(jnp.bfloat16)
    capacity = 2 * length // blocks
    own_targets = lax.dynamic_slice_in_dim(linear_row_index, block_index * length, length)
    target = own_targets // length
    owner_marks = (target[:, None] == lax.iota(jnp.int32, blocks)[None, :]).astype(jnp.int32)
    slot_rank = jnp.sum(owner_marks * (jnp.cumsum(owner_marks, axis=0) - 1), axis=1)
    send_slots = target * capacity + slot_rank

    def pack_slots(grad_rows):
        return (
            jnp.zeros((blocks * capacity, grad_rows.shape[1]), grad_rows.dtype)
            .at[send_slots]
            .set(grad_rows)
        )

    arrived = (
        lax.all_to_all(pack_slots(query_grad), "ctx", split_axis=0, concat_axis=0, tiled=True),
        lax.all_to_all(
            pack_slots(key_row_gradient), "ctx", split_axis=0, concat_axis=0, tiled=True
        ),
        lax.all_to_all(
            pack_slots(value_row_gradient), "ctx", split_axis=0, concat_axis=0, tiled=True
        ),
    )
    all_owners = linear_row_index.reshape(blocks, length)
    landing = all_owners // length == block_index
    landed_rank = jnp.cumsum(landing.astype(jnp.int32), axis=1) - 1
    source_slot = lax.iota(jnp.int32, blocks)[:, None] * capacity + landed_rank
    where_to = jnp.where(landing, all_owners % length, length)
    inverse = (
        jnp.zeros((length,), jnp.int32)
        .at[where_to.reshape(-1)]
        .set(source_slot.reshape(-1), mode="drop")
    )
    linear_query = arrived[0][inverse]
    linear_key = arrived[1][inverse]
    linear_value = arrived[2][inverse]
    result = (
        lax.all_to_all(linear_query, "head", split_axis=0, concat_axis=1, tiled=True),
        lax.all_to_all(linear_key, "head", split_axis=0, concat_axis=1, tiled=True),
        lax.all_to_all(linear_value, "head", split_axis=0, concat_axis=1, tiled=True),
    )
    return (result[0], result[1], result[2])


def solution(mesh):
    placed = (
        P("ctx", "head"),
        P("ctx", "head"),
        P("ctx", "head"),
        P("ctx", "head"),
        P("ctx", "head"),
        P("head", "ctx"),
        P(),
        P(),
    )
    return jax.shard_map(
        per_device,
        mesh=mesh,
        in_specs=placed,
        out_specs=(P(("ctx", "head"), None), P(("ctx", "head"), None), P(("ctx", "head"), None)),
        check_vma=False,
    )
```

profile of v0, /device:TPU:32, one launch (start us, length us, event | category | flops | bytes accessed | tf_op | source)
XLA Modules:
  0.0 360.1 jit_solution(3413833666730126142)
XLA Ops:
  2.5 15.1 %collective-permute-start = (bf16[256,128]{1,0:T(8,128)(2,1)}, bf16[256,128]{1,0:T(8,128)(2,1)S(1)}, u32[]{:S(2)}, u32[]{:S(2)}) collective-permute-start(bf16[256,128]{1,0:T(8,128)(2,1)} %param.9), channel_id=1, source_target_pairs={{0,8},{8,16},{16,24},{24,32},{32,40},{40,48},{48,56},{56,64},{64,7... | collective-permute-start | bytes 196616 | tf_op jit(solution)/shard_map/ppermute | solution.py:13
  22.9 2.1 collective-permute-start.6
  30.7 60.3 %scatter_custom_fusion.1 = s32[256]{0:T(256)S(1)} fusion(s32[16384]{0:T(1024)S(1)} %compare_select_fusion, s32[16384]{0:T(1024)S(1)} %add.156, s32[]{:T(128)} %constant.73.clone.1), kind=kCustom, calls=%fused_computation.185 | custom fusion | bytes 1028 | tf_op jit(solution)/shard_map/scatter | solution.py:159
  93.0 13.9 %collective-permute-start.2 = (bf16[256,128]{1,0:T(8,128)(2,1)S(1)}, bf16[256,128]{1,0:T(8,128)(2,1)S(1)}, u32[]{:S(2)}, u32[]{:S(2)}) collective-permute-start(bf16[256,128]{1,0:T(8,128)(2,1)S(1)} %collective-permute-done), channel_id=1, source_target_pairs={{0,8},{8,16},{16,24},{24,32},{32,40},{40,48},{48,56},{56,64},{64,7... | collective-permute-start | bytes 196616 | tf_op jit(solution)/shard_map/ppermute | solution.py:13
  107.8 2.3 collective-permute-start.4
  111.4 16.5 %collective-permute-start.7 = (f32[256,128]{1,0:T(8,128)S(1)}, f32[256,128]{1,0:T(8,128)S(1)}, u32[]{:S(2)}, u32[]{:S(2)}) collective-permute-start(f32[256,128]{1,0:T(8,128)S(1)} %fusion.45), channel_id=1, source_target_pairs={{504,0},{0,8},{8,16},{16,24},{24,32},{32,40},{40,48},{48,56},{56,6... | collective-permute-start | bytes 393224 | tf_op jit(solution)/shard_map/ppermute | solution.py:19
  131.0 4.1 %collective-permute-done.7 = f32[256,128]{1,0:T(8,128)S(1)} collective-permute-done((f32[256,128]{1,0:T(8,128)S(1)}, f32[256,128]{1,0:T(8,128)S(1)}, u32[]{:S(2)}, u32[]{:S(2)}) %collective-permute-start.7) | collective-permute-done | bytes 131104 | tf_op jit(solution)/shard_map/ppermute | solution.py:19
  137.4 18.8 %collective-permute-done.8 = f32[256,128]{1,0:T(8,128)S(1)} collective-permute-done((f32[256,128]{1,0:T(8,128)S(1)}, f32[256,128]{1,0:T(8,128)S(1)}, u32[]{:S(2)}, u32[]{:S(2)}) %collective-permute-start.8) | collective-permute-done | bytes 131104 | tf_op jit(solution)/shard_map/ppermute | solution.py:19
  158.4 12.3 %collective-permute-start.11 = (f32[256,128]{1,0:T(8,128)S(1)}, f32[256,128]{1,0:T(8,128)S(1)}, u32[]{:S(2)}, u32[]{:S(2)}) collective-permute-start(f32[256,128]{1,0:T(8,128)S(1)} %fusion.46), channel_id=1, source_target_pairs={{504,0},{0,8},{8,16},{16,24},{24,32},{32,40},{40,48},{48,56},{56,6... | collective-permute-start | bytes 393224 | tf_op jit(solution)/shard_map/ppermute | solution.py:19
  170.8 2.1 scatter_custom_fusion.2
  172.8 21.6 %all-to-all-start.2 = ((bf16[64,8,128]{2,1,0:T(8,128)(2,1)}), bf16[64,8,128]{2,1,0:T(8,128)(2,1)S(1)}, u32[]{:S(2)}, u32[]{:S(2)}) async-start(bf16[64,8,128]{2,1,0:T(8,128)(2,1)} %bitcast.50), calls=%async_computation.2 | async-start | bytes 262144 | tf_op jit(solution)/shard_map/all_to_all | solution.py:144
  197.0 21.8 %collective-permute-done.12 = f32[256,128]{1,0:T(8,128)S(1)} collective-permute-done((f32[256,128]{1,0:T(8,128)S(1)}, f32[256,128]{1,0:T(8,128)S(1)}, u32[]{:S(2)}, u32[]{:S(2)}) %collective-permute-start.12) | collective-permute-done | bytes 131104 | tf_op jit(solution)/shard_map/ppermute | solution.py:19
  220.8 12.4 %collective-permute-done.13 = bf16[256,128]{1,0:T(8,128)(2,1)S(1)} collective-permute-done((bf16[256,128]{1,0:T(8,128)(2,1)S(1)}, bf16[256,128]{1,0:T(8,128)(2,1)S(1)}, u32[]{:S(2)}, u32[]{:S(2)}) %collective-permute-start.13) | collective-permute-done | bytes 65568 | tf_op jit(solution)/shard_map/ppermute | solution.py:19
  235.0 15.5 %all-to-all-start.4 = ((bf16[64,8,128]{2,1,0:T(8,128)(2,1)}), bf16[64,8,128]{2,1,0:T(8,128)(2,1)S(1)}, u32[]{:S(2)}, u32[]{:S(2)}) async-start(bf16[64,8,128]{2,1,0:T(8,128)(2,1)} %bitcast.62), calls=%async_computation.4 | async-start | bytes 262144 | tf_op jit(solution)/shard_map/all_to_all | solution.py:147
  253.1 16.4 %all-to-all-done.4 = bf16[64,8,128]{2,1,0:T(8,128)(2,1)S(1)} async-done(((bf16[64,8,128]{2,1,0:T(8,128)(2,1)}), bf16[64,8,128]{2,1,0:T(8,128)(2,1)S(1)}, u32[]{:S(2)}, u32[]{:S(2)}) %all-to-all-start.4) | async-done | bytes 131104 | tf_op jit(solution)/shard_map/all_to_all | solution.py:147
  269.5 4.7 %all-to-all-start.3 = ((bf16[8,32,128]{2,1,0:T(8,128)(2,1)}), bf16[8,32,128]{2,1,0:T(8,128)(2,1)S(1)}, u32[]{:S(2)}, u32[]{:S(2)}) async-start(bf16[8,32,128]{2,1,0:T(8,128)(2,1)} %bitcast.52), calls=%async_computation.3 | async-start | bytes 131072 | tf_op jit(solution)/shard_map/all_to_all | solution.py:166
  274.6 2.3 scatter_custom_fusion
  276.9 6.5 %all-to-all-done.3 = bf16[8,32,128]{2,1,0:T(8,128)(2,1)S(1)} async-done(((bf16[8,32,128]{2,1,0:T(8,128)(2,1)}), bf16[8,32,128]{2,1,0:T(8,128)(2,1)S(1)}, u32[]{:S(2)}, u32[]{:S(2)}) %all-to-all-start.3) | async-done | bytes 65568 | tf_op jit(solution)/shard_map/all_to_all | solution.py:166
  283.5 4.6 %all-to-all-start = ((bf16[64,8,512]{2,1,0:T(8,128)(2,1)}), bf16[64,8,512]{2,1,0:T(8,128)(2,1)S(1)}, u32[]{:S(2)}, u32[]{:S(2)}) async-start(bf16[64,8,512]{2,1,0:T(8,128)(2,1)} %bitcast.40), calls=%async_computation | async-start | bytes 1048576 | tf_op jit(solution)/shard_map/all_to_all | solution.py:143
  289.6 36.7 %all-to-all-done = bf16[64,8,512]{2,1,0:T(8,128)(2,1)S(1)} async-done(((bf16[64,8,512]{2,1,0:T(8,128)(2,1)}), bf16[64,8,512]{2,1,0:T(8,128)(2,1)S(1)}, u32[]{:S(2)}, u32[]{:S(2)}) %all-to-all-start) | async-done | bytes 524320 | tf_op jit(solution)/shard_map/all_to_all | solution.py:143
  326.3 3.3 all-to-all-start.5
  331.4 7.4 %all-to-all-done.5 = bf16[8,32,128]{2,1,0:T(8,128)(2,1)S(1)} async-done(((bf16[8,32,128]{2,1,0:T(8,128)(2,1)}), bf16[8,32,128]{2,1,0:T(8,128)(2,1)S(1)}, u32[]{:S(2)}, u32[]{:S(2)}) %all-to-all-start.5) | async-done | bytes 65568 | tf_op jit(solution)/shard_map/all_to_all | solution.py:167
  338.8 5.0 %all-to-all-start.1 = ((bf16[8,32,512]{2,1,0:T(8,128)(2,1)}), bf16[8,32,512]{2,1,0:T(8,128)(2,1)S(1)}, u32[]{:S(2)}, u32[]{:S(2)}) async-start(bf16[8,32,512]{2,1,0:T(8,128)(2,1)} %bitcast.44), calls=%async_computation.1 | async-start | bytes 524288 | tf_op jit(solution)/shard_map/all_to_all | solution.py:165
  345.1 14.3 %all-to-all-done.1 = bf16[8,32,512]{2,1,0:T(8,128)(2,1)S(1)} async-done(((bf16[8,32,512]{2,1,0:T(8,128)(2,1)}), bf16[8,32,512]{2,1,0:T(8,128)(2,1)S(1)}, u32[]{:S(2)}, u32[]{:S(2)}) %all-to-all-start.1) | async-done | bytes 262176 | tf_op jit(solution)/shard_map/all_to_all | solution.py:165
  (118 shorter events, 38.8 us)
Async XLA Ops:
  0.6 20.1 %copy-start = (bf16[256,512]{1,0:T(8,128)(2,1)S(1)}, bf16[256,512]{1,0:T(8,128)(2,1)}, u32[]{:S(2)}) copy-start(bf16[256,512]{1,0:T(8,128)(2,1)} %param.8) | copy-start | bytes 786436
  0.6 90.4 %collective-permute-start.1 = (bf16[256,128]{1,0:T(8,128)(2,1)}, bf16[256,128]{1,0:T(8,128)(2,1)S(1)}, u32[]{:S(2)}, u32[]{:S(2)}) collective-permute-start(bf16[256,128]{1,0:T(8,128)(2,1)} %param.10), channel_id=1, source_target_pairs={{0,8},{8,16},{16,24},{24,32},{32,40},{40,48},{48,56},{56,64},{64,7... | collective-permute-start | bytes 196616 | tf_op jit(solution)/shard_map/ppermute | solution.py:13
  2.5 90.5 %collective-permute-start = (bf16[256,128]{1,0:T(8,128)(2,1)}, bf16[256,128]{1,0:T(8,128)(2,1)S(1)}, u32[]{:S(2)}, u32[]{:S(2)}) collective-permute-start(bf16[256,128]{1,0:T(8,128)(2,1)} %param.9), channel_id=1, source_target_pairs={{0,8},{8,16},{16,24},{24,32},{32,40},{40,48},{48,56},{56,64},{64,7... | collective-permute-start | bytes 196616 | tf_op jit(solution)/shard_map/ppermute | solution.py:13
  22.9 88.0 %collective-permute-start.6 = (f32[256,128]{1,0:T(8,128)S(1)}, f32[256,128]{1,0:T(8,128)S(1)}, u32[]{:S(2)}, u32[]{:S(2)}) collective-permute-start(f32[256,128]{1,0:T(8,128)S(1)} %convolution_bitcast_fusion.11), channel_id=1, source_target_pairs={{504,0},{0,8},{8,16},{16,24},{24,32},{32,40},{40,48},{48,56},{56,6... | collective-permute-start | bytes 393224 | tf_op jit(solution)/shard_map/ppermute | solution.py:19
  25.2 132.9 %collective-permute-start.10 = (f32[256,128]{1,0:T(8,128)S(1)}, f32[256,128]{1,0:T(8,128)S(1)}, u32[]{:S(2)}, u32[]{:S(2)}) collective-permute-start(f32[256,128]{1,0:T(8,128)S(1)} %convolution_bitcast_fusion.7), channel_id=1, source_target_pairs={{504,0},{0,8},{8,16},{16,24},{24,32},{32,40},{40,48},{48,56},{56,6... | collective-permute-start | bytes 393224 | tf_op jit(solution)/shard_map/ppermute | solution.py:19
  91.0 19.5 %collective-permute-start.3 = (bf16[256,128]{1,0:T(8,128)(2,1)S(1)}, bf16[256,128]{1,0:T(8,128)(2,1)S(1)}, u32[]{:S(2)}, u32[]{:S(2)}) collective-permute-start(bf16[256,128]{1,0:T(8,128)(2,1)S(1)} %collective-permute-done.1), channel_id=1, source_target_pairs={{0,8},{8,16},{16,24},{24,32},{32,40},{40,48},{48,56},{56,64},{64,7... | collective-permute-start | bytes 196616 | tf_op jit(solution)/shard_map/ppermute | solution.py:13
  93.0 14.3 %copy-start.7 = (bf16[256,128]{1,0:T(8,128)(2,1)}, bf16[256,128]{1,0:T(8,128)(2,1)S(1)}, u32[]{:S(2)}) copy-start(bf16[256,128]{1,0:T(8,128)(2,1)S(1)} %collective-permute-done) | copy-start | bytes 196612
  93.0 14.8 %collective-permute-start.2 = (bf16[256,128]{1,0:T(8,128)(2,1)S(1)}, bf16[256,128]{1,0:T(8,128)(2,1)S(1)}, u32[]{:S(2)}, u32[]{:S(2)}) collective-permute-start(bf16[256,128]{1,0:T(8,128)(2,1)S(1)} %collective-permute-done), channel_id=1, source_target_pairs={{0,8},{8,16},{16,24},{24,32},{32,40},{40,48},{48,56},{56,64},{64,7... | collective-permute-start | bytes 196616 | tf_op jit(solution)/shard_map/ppermute | solution.py:13
  107.8 22.1 %collective-permute-start.4 = (bf16[256,128]{1,0:T(8,128)(2,1)S(1)}, bf16[256,128]{1,0:T(8,128)(2,1)S(1)}, u32[]{:S(2)}, u32[]{:S(2)}) collective-permute-start(bf16[256,128]{1,0:T(8,128)(2,1)S(1)} %collective-permute-done.2), channel_id=1, source_target_pairs={{0,8},{8,16},{16,24},{24,32},{32,40},{40,48},{48,56},{56,64},{64,7... | collective-permute-start | bytes 196616 | tf_op jit(solution)/shard_map/ppermute | solution.py:13
  111.4 23.7 %collective-permute-start.7 = (f32[256,128]{1,0:T(8,128)S(1)}, f32[256,128]{1,0:T(8,128)S(1)}, u32[]{:S(2)}, u32[]{:S(2)}) collective-permute-start(f32[256,128]{1,0:T(8,128)S(1)} %fusion.45), channel_id=1, source_target_pairs={{504,0},{0,8},{8,16},{16,24},{24,32},{32,40},{40,48},{48,56},{56,6... | collective-permute-start | bytes 393224 | tf_op jit(solution)/shard_map/ppermute | solution.py:19
  127.9 2.8 collective-permute-start.5
  135.1 21.0 %collective-permute-start.8 = (f32[256,128]{1,0:T(8,128)S(1)}, f32[256,128]{1,0:T(8,128)S(1)}, u32[]{:S(2)}, u32[]{:S(2)}) collective-permute-start(f32[256,128]{1,0:T(8,128)S(1)} %add.159), channel_id=1, source_target_pairs={{504,0},{0,8},{8,16},{16,24},{24,32},{32,40},{40,48},{48,56},{56,6... | collective-permute-start | bytes 393224 | tf_op jit(solution)/shard_map/ppermute | solution.py:19
  156.2 14.5 %collective-permute-start.9 = (bf16[256,128]{1,0:T(8,128)(2,1)S(1)}, bf16[256,128]{1,0:T(8,128)(2,1)}, u32[]{:S(2)}, u32[]{:S(2)}) collective-permute-start(bf16[256,128]{1,0:T(8,128)(2,1)S(1)} %add_convert_fusion.1), channel_id=1, source_target_pairs={{24,0},{32,8},{40,16},{48,24},{56,32},{64,40},{72,48},{80,56},{88,... | collective-permute-start | bytes 196616 | tf_op jit(solution)/shard_map/ppermute | solution.py:19
  158.4 36.3 %collective-permute-start.11 = (f32[256,128]{1,0:T(8,128)S(1)}, f32[256,128]{1,0:T(8,128)S(1)}, u32[]{:S(2)}, u32[]{:S(2)}) collective-permute-start(f32[256,128]{1,0:T(8,128)S(1)} %fusion.46), channel_id=1, source_target_pairs={{504,0},{0,8},{8,16},{16,24},{24,32},{32,40},{40,48},{48,56},{56,6... | collective-permute-start | bytes 393224 | tf_op jit(solution)/shard_map/ppermute | solution.py:19
  172.8 62.1 %all-to-all-start.2 = ((bf16[64,8,128]{2,1,0:T(8,128)(2,1)}), bf16[64,8,128]{2,1,0:T(8,128)(2,1)S(1)}, u32[]{:S(2)}, u32[]{:S(2)}) async-start(bf16[64,8,128]{2,1,0:T(8,128)(2,1)} %bitcast.50), calls=%async_computation.2 | async-start | bytes 262144 | tf_op jit(solution)/shard_map/all_to_all | solution.py:144
  194.8 24.1 %collective-permute-start.12 = (f32[256,128]{1,0:T(8,128)S(1)}, f32[256,128]{1,0:T(8,128)S(1)}, u32[]{:S(2)}, u32[]{:S(2)}) collective-permute-start(f32[256,128]{1,0:T(8,128)S(1)} %add.162), channel_id=1, source_target_pairs={{504,0},{0,8},{8,16},{16,24},{24,32},{32,40},{40,48},{48,56},{56,6... | collective-permute-start | bytes 393224 | tf_op jit(solution)/shard_map/ppermute | solution.py:19
  197.0 53.5 %copy-start.4 = (f32[256,4,128]{0,2,1:T(8,128)S(1)}, f32[256,4,128]{0,2,1:T(8,128)}, u32[]{:S(2)}) copy-start(f32[256,4,128]{0,2,1:T(8,128)} %fusion.89) | copy-start | bytes 1572868
  218.9 14.3 %collective-permute-start.13 = (bf16[256,128]{1,0:T(8,128)(2,1)S(1)}, bf16[256,128]{1,0:T(8,128)(2,1)S(1)}, u32[]{:S(2)}, u32[]{:S(2)}) collective-permute-start(bf16[256,128]{1,0:T(8,128)(2,1)S(1)} %add_convert_fusion), channel_id=1, source_target_pairs={{24,0},{32,8},{40,16},{48,24},{56,32},{64,40},{72,48},{80,56},{88,... | collective-permute-start | bytes 196616 | tf_op jit(solution)/shard_map/ppermute | solution.py:19
  235.0 15.6 %copy-start.8 = (bf16[256,128]{1,0:T(8,128)(2,1)S(1)}, bf16[256,128]{1,0:T(8,128)(2,1)}, u32[]{:S(2)}) copy-start(bf16[256,128]{1,0:T(8,128)(2,1)} %copy-done.7) | copy-start | bytes 196612
  235.0 34.5 %all-to-all-start.4 = ((bf16[64,8,128]{2,1,0:T(8,128)(2,1)}), bf16[64,8,128]{2,1,0:T(8,128)(2,1)S(1)}, u32[]{:S(2)}, u32[]{:S(2)}) async-start(bf16[64,8,128]{2,1,0:T(8,128)(2,1)} %bitcast.62), calls=%async_computation.4 | async-start | bytes 262144 | tf_op jit(solution)/shard_map/all_to_all | solution.py:147
  269.5 13.9 %all-to-all-start.3 = ((bf16[8,32,128]{2,1,0:T(8,128)(2,1)}), bf16[8,32,128]{2,1,0:T(8,128)(2,1)S(1)}, u32[]{:S(2)}, u32[]{:S(2)}) async-start(bf16[8,32,128]{2,1,0:T(8,128)(2,1)} %bitcast.52), calls=%async_computation.3 | async-start | bytes 131072 | tf_op jit(solution)/shard_map/all_to_all | solution.py:166
  283.5 42.8 %all-to-all-start = ((bf16[64,8,512]{2,1,0:T(8,128)(2,1)}), bf16[64,8,512]{2,1,0:T(8,128)(2,1)S(1)}, u32[]{:S(2)}, u32[]{:S(2)}) async-start(bf16[64,8,512]{2,1,0:T(8,128)(2,1)} %bitcast.40), calls=%async_computation | async-start | bytes 1048576 | tf_op jit(solution)/shard_map/all_to_all | solution.py:143
  326.3 12.6 %all-to-all-start.5 = ((bf16[8,32,128]{2,1,0:T(8,128)(2,1)}), bf16[8,32,128]{2,1,0:T(8,128)(2,1)S(1)}, u32[]{:S(2)}, u32[]{:S(2)}) async-start(bf16[8,32,128]{2,1,0:T(8,128)(2,1)} %bitcast.64), calls=%async_computation.5 | async-start | bytes 131072 | tf_op jit(solution)/shard_map/all_to_all | solution.py:167
  338.8 20.5 %all-to-all-start.1 = ((bf16[8,32,512]{2,1,0:T(8,128)(2,1)}), bf16[8,32,512]{2,1,0:T(8,128)(2,1)S(1)}, u32[]{:S(2)}, u32[]{:S(2)}) async-start(bf16[8,32,512]{2,1,0:T(8,128)(2,1)} %bitcast.44), calls=%async_computation.1 | async-start | bytes 524288 | tf_op jit(solution)/shard_map/all_to_all | solution.py:165
  (12 other events, 24.4 us)
where the time goes:
time: 361 us; the launch traced here: 360 us
  waiting for transfers between devices  139 us (39%)
  starting transfers between devices  132 us (37%)
  local copies, waits for them, and re-layouts  76.9 us (21%)
  matrix products  6.8 us (2%)
  other arithmetic  4 us (1%)
    scatter x1, local copies, waits for them, and re-layouts, per_device(): inverse = jnp.zeros((length,), jnp.int32).at[where_to.reshape(-1)].set(so...  60.3 us
    ppermute x8, waiting for transfers between devices, shifted(): return lax.ppermute(block, axis, route)  57.1 us
    ppermute x8, starting transfers between devices, shifted(): return lax.ppermute(block, axis, route)  40.5 us
    ppermute x6, starting transfers between devices, from_behind(): return lax.ppermute(shard, axis, pairs)  37 us
    all_to_all x1, waiting for transfers between devices, per_device(): lax.all_to_all(pack_slots(query_grad), 'ctx', split_axis=0, concat_axis=0...  36.7 us
    all_to_all x1, starting transfers between devices, per_device(): lax.all_to_all(pack_slots(key_row_gradient), 'ctx', split_axis=0, concat_...  21.6 us
    all_to_all x1, waiting for transfers between devices, per_device(): lax.all_to_all(pack_slots(value_row_gradient), 'ctx', split_axis=0, conca...  16.4 us
    all_to_all x1, starting transfers between devices, per_device(): lax.all_to_all(pack_slots(value_row_gradient), 'ctx', split_axis=0, conca...  15.5 us
  transfers between devices with their start and end apart: 20, of which 11 were waited for; matrix products, arithmetic and copies ran while one was open for 23% of the time, Pallas kernels for 0%

commit v1 on v0

--- a/solution.py
+++ b/solution.py
@@ -5,6 +5,13 @@
 
 HEAD_SIZE = 128
 DOC_BLOCKS = 3
+
+
+def _recast_lanes(mine_x):
+    row_out = jnp.stack(jnp.split(mine_x, lax.psum(1, "head"), axis=0), axis=0)
+    frame_out = lax.all_to_all(row_out, concat_axis=0, split_axis=0, axis_name="head")
+    tall = jnp.concatenate(frame_out, axis=1)
+    return tall
 
 
 def from_behind(shard, axis, by):
@@ -163,7 +170,7 @@
     linear_value = arrived[2][inverse]
     result = (
         lax.all_to_all(linear_query, "head", split_axis=0, concat_axis=1, tiled=True),
-        lax.all_to_all(linear_key, "head", split_axis=0, concat_axis=1, tiled=True),
+        _recast_lanes(linear_key),
         lax.all_to_all(linear_value, "head", split_axis=0, concat_axis=1, tiled=True),
     )
     return (result[0], result[1], result[2])

time: 361 us -> 345 us (0.956)
  waiting for transfers between devices: 139 us -> 101 us
  starting transfers between devices: 132 us -> 151 us
    ppermute x8, waiting for transfers between devices: 57.1 us -> 23.3 us  [shifted(): return lax.ppermute(block, axis, route)]
    ppermute x8, starting transfers between devices: 40.5 us -> 54.2 us  [shifted(): return lax.ppermute(block, axis, route)]
    all_to_all x1, starting transfers between devices: 15.5 us -> 20.2 us  [per_device(): lax.all_to_all(pack_slots(value_row_gradient), 'ctx', split_axis=0, conca...]
    all_to_all x1, waiting for transfers between devices: 16.4 us -> 12.3 us  [per_device(): lax.all_to_all(pack_slots(value_row_gradient), 'ctx', split_axis=0, conca...]
    unnamed x34 -> x31, local copies, waits for them, and re-layouts: 2.71 us -> 6.35 us
  transfers between devices with their start and end apart: 20 -> 20, of which waited for: 11 -> 9; matrix products, arithmetic and copies ran while one was open for 23% -> 25% of each run, Pallas kernels for 0% -> 0%
where the time goes in v1:
time: 345 us; the launch traced here: 344 us
  starting transfers between devices  151 us (44%)
  waiting for transfers between devices  101 us (29%)
  local copies, waits for them, and re-layouts  80.5 us (23%)
  matrix products  5.96 us (2%)
  other arithmetic  4.01 us (1%)
    scatter x1, local copies, waits for them, and re-layouts, per_device(): inverse = jnp.zeros((length,), jnp.int32).at[where_to.reshape(-1)].set(so...  60.3 us
    ppermute x8, starting transfers between devices, shifted(): return lax.ppermute(block, axis, route)  54.2 us
    all_to_all x1, waiting for transfers between devices, per_device(): lax.all_to_all(pack_slots(query_grad), 'ctx', split_axis=0, concat_axis=0...  36.7 us
    ppermute x6, starting transfers between devices, from_behind(): return lax.ppermute(shard, axis, pairs)  36.6 us
    ppermute x8, waiting for transfers between devices, shifted(): return lax.ppermute(block, axis, route)  23.3 us
    all_to_all x1, starting transfers between devices, per_device(): lax.all_to_all(pack_slots(key_row_gradient), 'ctx', split_axis=0, concat_...  20.3 us
    all_to_all x1, starting transfers between devices, per_device(): lax.all_to_all(pack_slots(value_row_gradient), 'ctx', split_axis=0, conca...  20.2 us
    all_to_all x1, waiting for transfers between devices, per_device(): lax.all_to_all(linear_query, 'head', split_axis=0, concat_axis=1, tiled=T...  14.3 us
  transfers between devices with their start and end apart: 20, of which 9 were waited for; matrix products, arithmetic and copies ran while one was open for 25% of the time, Pallas kernels for 0%

profile of v1, /device:TPU:32, one launch (start us, length us, event | category | flops | bytes accessed | tf_op | source)
XLA Modules:
  0.0 344.2 jit_solution(291650036474579016)
XLA Ops:
  2.5 15.1 %collective-permute-start = (bf16[256,128]{1,0:T(8,128)(2,1)}, bf16[256,128]{1,0:T(8,128)(2,1)S(1)}, u32[]{:S(2)}, u32[]{:S(2)}) collective-permute-start(bf16[256,128]{1,0:T(8,128)(2,1)} %param.9), channel_id=1, source_target_pairs={{0,8},{8,16},{16,24},{24,32},{32,40},{40,48},{48,56},{56,64},{64,7... | collective-permute-start | bytes 196616 | tf_op jit(solution)/shard_map/ppermute | solution.py:20
  22.9 2.1 collective-permute-start.6
  29.9 60.3 %scatter_custom_fusion.1 = s32[256]{0:T(256)S(1)} fusion(s32[16384]{0:T(1024)S(1)} %compare_select_fusion, s32[16384]{0:T(1024)S(1)} %add.156, s32[]{:T(128)} %constant.73.clone.1), kind=kCustom, calls=%fused_computation.201 | custom fusion | bytes 1028 | tf_op jit(solution)/shard_map/scatter | solution.py:166
  92.2 13.8 %collective-permute-start.2 = (bf16[256,128]{1,0:T(8,128)(2,1)S(1)}, bf16[256,128]{1,0:T(8,128)(2,1)S(1)}, u32[]{:S(2)}, u32[]{:S(2)}) collective-permute-start(bf16[256,128]{1,0:T(8,128)(2,1)S(1)} %collective-permute-done), channel_id=1, source_target_pairs={{0,8},{8,16},{16,24},{24,32},{32,40},{40,48},{48,56},{56,64},{64,7... | collective-permute-start | bytes 196616 | tf_op jit(solution)/shard_map/ppermute | solution.py:20
  112.5 14.6 %collective-permute-start.11 = (f32[256,128]{1,0:T(8,128)S(1)}, f32[256,128]{1,0:T(8,128)S(1)}, u32[]{:S(2)}, u32[]{:S(2)}) collective-permute-start(f32[256,128]{1,0:T(8,128)S(1)} %fusion.46), channel_id=1, source_target_pairs={{504,0},{0,8},{8,16},{16,24},{24,32},{32,40},{40,48},{48,56},{56,6... | collective-permute-start | bytes 393224 | tf_op jit(solution)/shard_map/ppermute | solution.py:26
  130.2 3.5 %collective-permute-start.8 = (f32[256,128]{1,0:T(8,128)S(1)}, f32[256,128]{1,0:T(8,128)S(1)}, u32[]{:S(2)}, u32[]{:S(2)}) collective-permute-start(f32[256,128]{1,0:T(8,128)S(1)} %add.159), channel_id=1, source_target_pairs={{504,0},{0,8},{8,16},{16,24},{24,32},{32,40},{40,48},{48,56},{56,6... | collective-permute-start | bytes 393224 | tf_op jit(solution)/shard_map/ppermute | solution.py:26
  134.0 15.5 %collective-permute-done.8 = f32[256,128]{1,0:T(8,128)S(1)} collective-permute-done((f32[256,128]{1,0:T(8,128)S(1)}, f32[256,128]{1,0:T(8,128)S(1)}, u32[]{:S(2)}, u32[]{:S(2)}) %collective-permute-start.8) | collective-permute-done | bytes 131104 | tf_op jit(solution)/shard_map/ppermute | solution.py:26
  149.5 10.5 %collective-permute-start.9 = (bf16[256,128]{1,0:T(8,128)(2,1)S(1)}, bf16[256,128]{1,0:T(8,128)(2,1)}, u32[]{:S(2)}, u32[]{:S(2)}) collective-permute-start(bf16[256,128]{1,0:T(8,128)(2,1)S(1)} %add_convert_fusion.1), channel_id=1, source_target_pairs={{24,0},{32,8},{40,16},{48,24},{56,32},{64,40},{72,48},{80,56},{88,... | collective-permute-start | bytes 196616 | tf_op jit(solution)/shard_map/ppermute | solution.py:26
  160.3 12.9 %collective-permute-start.12 = (f32[256,128]{1,0:T(8,128)S(1)}, f32[256,128]{1,0:T(8,128)S(1)}, u32[]{:S(2)}, u32[]{:S(2)}) collective-permute-start(f32[256,128]{1,0:T(8,128)S(1)} %add.162), channel_id=1, source_target_pairs={{504,0},{0,8},{8,16},{16,24},{24,32},{32,40},{40,48},{48,56},{56,6... | collective-permute-start | bytes 393224 | tf_op jit(solution)/shard_map/ppermute | solution.py:26
  173.3 2.1 scatter_custom_fusion.2
  175.3 20.3 %all-to-all-start.2 = ((bf16[64,8,128]{2,1,0:T(8,128)(2,1)}), bf16[64,8,128]{2,1,0:T(8,128)(2,1)S(1)}, u32[]{:S(2)}, u32[]{:S(2)}) async-start(bf16[64,8,128]{2,1,0:T(8,128)(2,1)} %bitcast.50), calls=%async_computation.2 | async-start | bytes 262144 | tf_op jit(solution)/shard_map/all_to_all | solution.py:151
  196.0 6.8 %collective-permute-start.13 = (bf16[256,128]{1,0:T(8,128)(2,1)S(1)}, bf16[256,128]{1,0:T(8,128)(2,1)S(1)}, u32[]{:S(2)}, u32[]{:S(2)}) collective-permute-start(bf16[256,128]{1,0:T(8,128)(2,1)S(1)} %add_convert_fusion), channel_id=1, source_target_pairs={{24,0},{32,8},{40,16},{48,24},{56,32},{64,40},{72,48},{80,56},{88,... | collective-permute-start | bytes 196616 | tf_op jit(solution)/shard_map/ppermute | solution.py:26
  203.1 7.8 %collective-permute-done.13 = bf16[256,128]{1,0:T(8,128)(2,1)S(1)} collective-permute-done((bf16[256,128]{1,0:T(8,128)(2,1)S(1)}, bf16[256,128]{1,0:T(8,128)(2,1)S(1)}, u32[]{:S(2)}, u32[]{:S(2)}) %collective-permute-start.13) | collective-permute-done | bytes 65568 | tf_op jit(solution)/shard_map/ppermute | solution.py:26
  213.1 20.2 %all-to-all-start.4 = ((bf16[64,8,128]{2,1,0:T(8,128)(2,1)}), bf16[64,8,128]{2,1,0:T(8,128)(2,1)S(1)}, u32[]{:S(2)}, u32[]{:S(2)}) async-start(bf16[64,8,128]{2,1,0:T(8,128)(2,1)} %bitcast.69), calls=%async_computation.4 | async-start | bytes 262144 | tf_op jit(solution)/shard_map/all_to_all | solution.py:154
  239.0 12.3 %all-to-all-done.4 = bf16[64,8,128]{2,1,0:T(8,128)(2,1)S(1)} async-done(((bf16[64,8,128]{2,1,0:T(8,128)(2,1)}), bf16[64,8,128]{2,1,0:T(8,128)(2,1)S(1)}, u32[]{:S(2)}, u32[]{:S(2)}) %all-to-all-start.4) | async-done | bytes 131104 | tf_op jit(solution)/shard_map/all_to_all | solution.py:154
  251.4 5.7 %all-to-all-start.3 = ((bf16[8,32,128]{2,1,0:T(8,128)(2,1)}), bf16[8,32,128]{2,1,0:T(8,128)(2,1)S(1)}, u32[]{:S(2)}, u32[]{:S(2)}) async-start(bf16[8,32,128]{2,1,0:T(8,128)(2,1)} %constant_dynamic-update-slice_fusion), calls=%async_computation.3 | async-start | bytes 131072 | tf_op jit(solution)/shard_map/all_to_all | solution.py:12
  257.5 2.3 scatter_custom_fusion
  259.8 6.5 %all-to-all-done.3 = bf16[8,32,128]{2,1,0:T(8,128)(2,1)S(1)} async-done(((bf16[8,32,128]{2,1,0:T(8,128)(2,1)}), bf16[8,32,128]{2,1,0:T(8,128)(2,1)S(1)}, u32[]{:S(2)}, u32[]{:S(2)}) %all-to-all-start.3) | async-done | bytes 65568 | tf_op jit(solution)/shard_map/all_to_all | solution.py:12
  266.3 5.8 %all-to-all-start = ((bf16[64,8,512]{2,1,0:T(8,128)(2,1)}), bf16[64,8,512]{2,1,0:T(8,128)(2,1)S(1)}, u32[]{:S(2)}, u32[]{:S(2)}) async-start(bf16[64,8,512]{2,1,0:T(8,128)(2,1)} %bitcast.40), calls=%async_computation | async-start | bytes 1048576 | tf_op jit(solution)/shard_map/all_to_all | solution.py:150
  273.6 36.7 %all-to-all-done = bf16[64,8,512]{2,1,0:T(8,128)(2,1)S(1)} async-done(((bf16[64,8,512]{2,1,0:T(8,128)(2,1)}), bf16[64,8,512]{2,1,0:T(8,128)(2,1)S(1)}, u32[]{:S(2)}, u32[]{:S(2)}) %all-to-all-start) | async-done | bytes 524320 | tf_op jit(solution)/shard_map/all_to_all | solution.py:150
  310.4 3.3 all-to-all-start.5
  315.5 7.4 %all-to-all-done.5 = bf16[8,32,128]{2,1,0:T(8,128)(2,1)S(1)} async-done(((bf16[8,32,128]{2,1,0:T(8,128)(2,1)}), bf16[8,32,128]{2,1,0:T(8,128)(2,1)S(1)}, u32[]{:S(2)}, u32[]{:S(2)}) %all-to-all-start.5) | async-done | bytes 65568 | tf_op jit(solution)/shard_map/all_to_all | solution.py:174
  322.9 5.0 %all-to-all-start.1 = ((bf16[8,32,512]{2,1,0:T(8,128)(2,1)}), bf16[8,32,512]{2,1,0:T(8,128)(2,1)S(1)}, u32[]{:S(2)}, u32[]{:S(2)}) async-start(bf16[8,32,512]{2,1,0:T(8,128)(2,1)} %bitcast.44), calls=%async_computation.1 | async-start | bytes 524288 | tf_op jit(solution)/shard_map/all_to_all | solution.py:172
  329.1 14.3 %all-to-all-done.1 = bf16[8,32,512]{2,1,0:T(8,128)(2,1)S(1)} async-done(((bf16[8,32,512]{2,1,0:T(8,128)(2,1)}), bf16[8,32,512]{2,1,0:T(8,128)(2,1)S(1)}, u32[]{:S(2)}, u32[]{:S(2)}) %all-to-all-start.1) | async-done | bytes 262176 | tf_op jit(solution)/shard_map/all_to_all | solution.py:172
  (116 shorter events, 38.0 us)
Async XLA Ops:
  0.6 20.1 %copy-start = (bf16[256,512]{1,0:T(8,128)(2,1)S(1)}, bf16[256,512]{1,0:T(8,128)(2,1)}, u32[]{:S(2)}) copy-start(bf16[256,512]{1,0:T(8,128)(2,1)} %param.8) | copy-start | bytes 786436
  0.6 89.6 %collective-permute-start.1 = (bf16[256,128]{1,0:T(8,128)(2,1)}, bf16[256,128]{1,0:T(8,128)(2,1)S(1)}, u32[]{:S(2)}, u32[]{:S(2)}) collective-permute-start(bf16[256,128]{1,0:T(8,128)(2,1)} %param.10), channel_id=1, source_target_pairs={{0,8},{8,16},{16,24},{24,32},{32,40},{40,48},{48,56},{56,64},{64,7... | collective-permute-start | bytes 196616 | tf_op jit(solution)/shard_map/ppermute | solution.py:20
  2.5 89.7 %collective-permute-start = (bf16[256,128]{1,0:T(8,128)(2,1)}, bf16[256,128]{1,0:T(8,128)(2,1)S(1)}, u32[]{:S(2)}, u32[]{:S(2)}) collective-permute-start(bf16[256,128]{1,0:T(8,128)(2,1)} %param.9), channel_id=1, source_target_pairs={{0,8},{8,16},{16,24},{24,32},{32,40},{40,48},{48,56},{56,64},{64,7... | collective-permute-start | bytes 196616 | tf_op jit(solution)/shard_map/ppermute | solution.py:20
  22.8 4.3 %copy-start.2 = (s32[16384]{0:T(1024)S(1)}, s32[16384]{0:T(1024)}, u32[]{:S(2)}) copy-start(s32[16384]{0:T(1024)} %param.15) | copy-start | bytes 196612
  22.9 84.2 %collective-permute-start.6 = (f32[256,128]{1,0:T(8,128)S(1)}, f32[256,128]{1,0:T(8,128)S(1)}, u32[]{:S(2)}, u32[]{:S(2)}) collective-permute-start(f32[256,128]{1,0:T(8,128)S(1)} %convolution_bitcast_fusion.11), channel_id=1, source_target_pairs={{504,0},{0,8},{8,16},{16,24},{24,32},{32,40},{40,48},{48,56},{56,6... | collective-permute-start | bytes 393224 | tf_op jit(solution)/shard_map/ppermute | solution.py:26
  25.2 87.0 %collective-permute-start.10 = (f32[256,128]{1,0:T(8,128)S(1)}, f32[256,128]{1,0:T(8,128)S(1)}, u32[]{:S(2)}, u32[]{:S(2)}) collective-permute-start(f32[256,128]{1,0:T(8,128)S(1)} %convolution_bitcast_fusion.7), channel_id=1, source_target_pairs={{504,0},{0,8},{8,16},{16,24},{24,32},{32,40},{40,48},{48,56},{56,6... | collective-permute-start | bytes 393224 | tf_op jit(solution)/shard_map/ppermute | solution.py:26
  90.3 21.3 %collective-permute-start.3 = (bf16[256,128]{1,0:T(8,128)(2,1)S(1)}, bf16[256,128]{1,0:T(8,128)(2,1)S(1)}, u32[]{:S(2)}, u32[]{:S(2)}) collective-permute-start(bf16[256,128]{1,0:T(8,128)(2,1)S(1)} %collective-permute-done.1), channel_id=1, source_target_pairs={{0,8},{8,16},{16,24},{24,32},{32,40},{40,48},{48,56},{56,64},{64,7... | collective-permute-start | bytes 196616 | tf_op jit(solution)/shard_map/ppermute | solution.py:20
  92.2 17.1 %collective-permute-start.2 = (bf16[256,128]{1,0:T(8,128)(2,1)S(1)}, bf16[256,128]{1,0:T(8,128)(2,1)S(1)}, u32[]{:S(2)}, u32[]{:S(2)}) collective-permute-start(bf16[256,128]{1,0:T(8,128)(2,1)S(1)} %collective-permute-done), channel_id=1, source_target_pairs={{0,8},{8,16},{16,24},{24,32},{32,40},{40,48},{48,56},{56,64},{64,7... | collective-permute-start | bytes 196616 | tf_op jit(solution)/shard_map/ppermute | solution.py:20
  107.3 22.9 %collective-permute-start.7 = (f32[256,128]{1,0:T(8,128)S(1)}, f32[256,128]{1,0:T(8,128)S(1)}, u32[]{:S(2)}, u32[]{:S(2)}) collective-permute-start(f32[256,128]{1,0:T(8,128)S(1)} %fusion.45), channel_id=1, source_target_pairs={{504,0},{0,8},{8,16},{16,24},{24,32},{32,40},{40,48},{48,56},{56,6... | collective-permute-start | bytes 393224 | tf_op jit(solution)/shard_map/ppermute | solution.py:26
  109.3 19.7 %collective-permute-start.4 = (bf16[256,128]{1,0:T(8,128)(2,1)S(1)}, bf16[256,128]{1,0:T(8,128)(2,1)S(1)}, u32[]{:S(2)}, u32[]{:S(2)}) collective-permute-start(bf16[256,128]{1,0:T(8,128)(2,1)S(1)} %collective-permute-done.2), channel_id=1, source_target_pairs={{0,8},{8,16},{16,24},{24,32},{32,40},{40,48},{48,56},{56,64},{64,7... | collective-permute-start | bytes 196616 | tf_op jit(solution)/shard_map/ppermute | solution.py:20
  112.5 47.8 %collective-permute-start.11 = (f32[256,128]{1,0:T(8,128)S(1)}, f32[256,128]{1,0:T(8,128)S(1)}, u32[]{:S(2)}, u32[]{:S(2)}) collective-permute-start(f32[256,128]{1,0:T(8,128)S(1)} %fusion.46), channel_id=1, source_target_pairs={{504,0},{0,8},{8,16},{16,24},{24,32},{32,40},{40,48},{48,56},{56,6... | collective-permute-start | bytes 393224 | tf_op jit(solution)/shard_map/ppermute | solution.py:26
  127.1 2.8 collective-permute-start.5
  130.2 19.2 %collective-permute-start.8 = (f32[256,128]{1,0:T(8,128)S(1)}, f32[256,128]{1,0:T(8,128)S(1)}, u32[]{:S(2)}, u32[]{:S(2)}) collective-permute-start(f32[256,128]{1,0:T(8,128)S(1)} %add.159), channel_id=1, source_target_pairs={{504,0},{0,8},{8,16},{16,24},{24,32},{32,40},{40,48},{48,56},{56,6... | collective-permute-start | bytes 393224 | tf_op jit(solution)/shard_map/ppermute | solution.py:26
  149.5 23.8 %collective-permute-start.9 = (bf16[256,128]{1,0:T(8,128)(2,1)S(1)}, bf16[256,128]{1,0:T(8,128)(2,1)}, u32[]{:S(2)}, u32[]{:S(2)}) collective-permute-start(bf16[256,128]{1,0:T(8,128)(2,1)S(1)} %add_convert_fusion.1), channel_id=1, source_target_pairs={{24,0},{32,8},{40,16},{48,24},{56,32},{64,40},{72,48},{80,56},{88,... | collective-permute-start | bytes 196616 | tf_op jit(solution)/shard_map/ppermute | solution.py:26
  160.3 35.6 %collective-permute-start.12 = (f32[256,128]{1,0:T(8,128)S(1)}, f32[256,128]{1,0:T(8,128)S(1)}, u32[]{:S(2)}, u32[]{:S(2)}) collective-permute-start(f32[256,128]{1,0:T(8,128)S(1)} %add.162), channel_id=1, source_target_pairs={{504,0},{0,8},{8,16},{16,24},{24,32},{32,40},{40,48},{48,56},{56,6... | collective-permute-start | bytes 393224 | tf_op jit(solution)/shard_map/ppermute | solution.py:26
  175.3 37.8 %all-to-all-start.2 = ((bf16[64,8,128]{2,1,0:T(8,128)(2,1)}), bf16[64,8,128]{2,1,0:T(8,128)(2,1)S(1)}, u32[]{:S(2)}, u32[]{:S(2)}) async-start(bf16[64,8,128]{2,1,0:T(8,128)(2,1)} %bitcast.50), calls=%async_computation.2 | async-start | bytes 262144 | tf_op jit(solution)/shard_map/all_to_all | solution.py:151
  195.9 6.9 %copy-start.5 = (bf16[256,128]{1,0:T(8,128)(2,1)S(1)}, bf16[256,128]{1,0:T(8,128)(2,1)}, u32[]{:S(2)}) copy-start(bf16[256,128]{1,0:T(8,128)(2,1)} %copy-done.4) | copy-start | bytes 196612
  196.0 14.9 %collective-permute-start.13 = (bf16[256,128]{1,0:T(8,128)(2,1)S(1)}, bf16[256,128]{1,0:T(8,128)(2,1)S(1)}, u32[]{:S(2)}, u32[]{:S(2)}) collective-permute-start(bf16[256,128]{1,0:T(8,128)(2,1)S(1)} %add_convert_fusion), channel_id=1, source_target_pairs={{24,0},{32,8},{40,16},{48,24},{56,32},{64,40},{72,48},{80,56},{88,... | collective-permute-start | bytes 196616 | tf_op jit(solution)/shard_map/ppermute | solution.py:26
  213.1 38.2 %all-to-all-start.4 = ((bf16[64,8,128]{2,1,0:T(8,128)(2,1)}), bf16[64,8,128]{2,1,0:T(8,128)(2,1)S(1)}, u32[]{:S(2)}, u32[]{:S(2)}) async-start(bf16[64,8,128]{2,1,0:T(8,128)(2,1)} %bitcast.69), calls=%async_computation.4 | async-start | bytes 262144 | tf_op jit(solution)/shard_map/all_to_all | solution.py:154
  239.0 18.0 %copy-start.7 = (bf16[256,128]{1,0:T(8,128)(2,1)S(1)}, bf16[256,128]{1,0:T(8,128)(2,1)}, u32[]{:S(2)}) copy-start(bf16[256,128]{1,0:T(8,128)(2,1)} %copy-done.6) | copy-start | bytes 196612
  251.4 15.0 %all-to-all-start.3 = ((bf16[8,32,128]{2,1,0:T(8,128)(2,1)}), bf16[8,32,128]{2,1,0:T(8,128)(2,1)S(1)}, u32[]{:S(2)}, u32[]{:S(2)}) async-start(bf16[8,32,128]{2,1,0:T(8,128)(2,1)} %constant_dynamic-update-slice_fusion), calls=%async_computation.3 | async-start | bytes 131072 | tf_op jit(solution)/shard_map/all_to_all | solution.py:12
  266.3 44.0 %all-to-all-start = ((bf16[64,8,512]{2,1,0:T(8,128)(2,1)}), bf16[64,8,512]{2,1,0:T(8,128)(2,1)S(1)}, u32[]{:S(2)}, u32[]{:S(2)}) async-start(bf16[64,8,512]{2,1,0:T(8,128)(2,1)} %bitcast.40), calls=%async_computation | async-start | bytes 1048576 | tf_op jit(solution)/shard_map/all_to_all | solution.py:150
  310.4 12.6 %all-to-all-start.5 = ((bf16[8,32,128]{2,1,0:T(8,128)(2,1)}), bf16[8,32,128]{2,1,0:T(8,128)(2,1)S(1)}, u32[]{:S(2)}, u32[]{:S(2)}) async-start(bf16[8,32,128]{2,1,0:T(8,128)(2,1)} %bitcast.71), calls=%async_computation.5 | async-start | bytes 131072 | tf_op jit(solution)/shard_map/all_to_all | solution.py:174
  322.9 20.5 %all-to-all-start.1 = ((bf16[8,32,512]{2,1,0:T(8,128)(2,1)}), bf16[8,32,512]{2,1,0:T(8,128)(2,1)S(1)}, u32[]{:S(2)}, u32[]{:S(2)}) async-start(bf16[8,32,512]{2,1,0:T(8,128)(2,1)} %bitcast.44), calls=%async_computation.1 | async-start | bytes 524288 | tf_op jit(solution)/shard_map/all_to_all | solution.py:172
  (7 other events, 7.2 us)
